TPU v7x, 32 devices: a whole 2x2x4 slice. The times are simulated.
32 devices in a mesh: rep: 2 (over x), member: 4 (over y, core), tp: 4 (over z).
Axes of the slice: x: 2, y: 2, z: 4, core: 2. Of those that a mesh axis runs over, the one named last changes fastest.
Arguments:
- states: bfloat16 [4096, 1024], P(('rep', 'member', 'tp')), parts along dimension 0, may hold values from -6 to 6
- member_of: int32 [4096, 1], P(('rep', 'member', 'tp')), parts along dimension 0, may hold values from 0 to 1; in each aligned block of 128 rows (0 to 127, 128 to 255, ...) at most 128 rows name the same one
- place: int32 [4096], P(('rep', 'member', 'tp')), parts along dimension 0, may hold values from 0 to 2047, as said below
- norm_gain: float32 [2, 1024], replicated, may hold values from 0.5 to 2
- w_up: bfloat16 [4, 1024, 2048], P('member', None, 'tp'), may hold values from -0.1875 to 0.1875
- w_down: bfloat16 [4, 2048, 1024], P('member', 'tp'), may hold values from -0.09375 to 0.09375
- policy_gain: float32 [1024], replicated, may hold values from 0.5 to 2
- w_policy: bfloat16 [1024, 128], replicated, may hold values from -0.1875 to 0.1875
Outputs:
- imagined: bfloat16 [4096, 1024], P(('rep', 'member', 'tp')), parts along dimension 0
- action: bfloat16 [4096, 128], P(('rep', 'member', 'tp')), parts along dimension 0
There are 2 independent parts, one for each index of `rep`. A program takes and returns all parts, laid end to end along the dimension named above; an argument that names none is the same for every part. Nothing has to cross between parts.
Inputs may be any that keep to these rules, and one draw needn't show every extreme that they name: `member_of`: at most 128 of the rows of one device name any one member, and that count is reached on some device. `place`: A permutation of the 2048 learner positions; learner device k holds positions k * 128 to (k + 1) * 128 - 1, and the rows of each device go exactly 8 to every learner device.
All inputs are finite; a program needn't handle non-finite values.
Results may differ from a plain program's by a relative error of at most 0.0069.
Values may be sent and summed in bfloat16 or wider, within the bound.
No kernel may reach another device: no remote copies, remote signals or barrier semaphores. Data moves between devices by JAX's collectives and lax.ppermute only.
A program may use at most 128 MiB of HBM per device.

v0:
```python
import jax
import jax.numpy as jnp
from jax import lax
from jax.sharding import PartitionSpec as P


def from_partner(value, axis, distance):
    return lax.ppermute(value, axis, [(i, i ^ 1 << distance) for i in range(lax.axis_size(axis))])


def rms_scale(values, gain):
    mean_square = jnp.mean(values * values, axis=-1, keepdims=True)
    return values * lax.rsqrt(mean_square + 1e-06) * gain


def running_rank(member_hits):
    return jnp.sum((jnp.cumsum(member_hits, axis=0) - member_hits) * member_hits, axis=1)


def local(states, member_of, place, norm_gain, w_up, w_down, policy_gain, w_policy):
    n_member = lax.axis_size("member")
    n_tp = lax.axis_size("tp")
    n_dev = n_member * n_tp
    group_width = 2 * n_tp
    member_total = n_member // 2
    rows_here = states.shape[0]
    feature_width = states.shape[1]
    slot_count = 2 * rows_here // n_dev
    member = member_of[:, 0]
    member_hits = (member[:, None] == jnp.arange(member_total, dtype=jnp.int32)[None, :]).astype(
        jnp.int32
    )
    earlier = running_rank(member_hits)
    target = (member * group_width + earlier % group_width) * slot_count + earlier // group_width
    picker = (jnp.arange(n_dev * slot_count, dtype=jnp.int32)[:, None] == target[None, :]).astype(
        jnp.bfloat16
    )
    outgoing = jnp.dot(picker, states, preferred_element_type=jnp.float32).astype(jnp.bfloat16)
    arrived = lax.all_to_all(
        outgoing.reshape(n_dev, slot_count, feature_width),
        ("member", "tp"),
        split_axis=0,
        concat_axis=0,
        tiled=True,
    )
    arrived = arrived.reshape(n_dev * slot_count, feature_width)
    arrived_count = arrived.shape[0]
    own_member = lax.axis_index("member") // 2
    gain_here = lax.dynamic_index_in_dim(norm_gain, own_member, 0, keepdims=False)
    normed = rms_scale(arrived.astype(jnp.float32), gain_here).astype(jnp.bfloat16)
    partner_normed = from_partner(normed, "member", 0)
    both_rows = jnp.concatenate([normed, partner_normed], axis=0)
    up_local = w_up[0]
    down_local = w_down[0]
    hidden = jax.nn.gelu(
        jnp.dot(
            lax.all_gather(both_rows, "tp", axis=0, tiled=True),
            up_local,
            preferred_element_type=jnp.float32,
        )
    ).astype(jnp.bfloat16)
    half_change = lax.psum_scatter(
        jnp.dot(hidden, down_local, preferred_element_type=jnp.float32),
        "tp",
        scatter_dimension=0,
        tiled=True,
    )
    partner_part = from_partner(half_change[arrived_count:], "member", 0)
    change = half_change[:arrived_count] + partner_part
    predicted = (arrived.astype(jnp.float32) + change).astype(jnp.bfloat16)
    returned = lax.all_to_all(
        predicted.reshape(n_dev, slot_count, feature_width),
        ("member", "tp"),
        split_axis=0,
        concat_axis=0,
        tiled=True,
    )
    returned = returned.reshape(n_dev * slot_count, feature_width)
    own_rows = jnp.einsum("sr,sd->rd", picker, returned, preferred_element_type=jnp.float32).astype(
        jnp.bfloat16
    )
    per_learner = rows_here // n_dev
    learner = place // rows_here
    spot_index = place % rows_here
    learner_hits = (learner[:, None] == jnp.arange(n_dev, dtype=jnp.int32)[None, :]).astype(
        jnp.int32
    )
    lane_index = learner * per_learner + running_rank(learner_hits)
    placer = jnp.arange(rows_here, dtype=jnp.int32)[:, None] == lane_index[None, :]
    packed = jnp.dot(
        placer.astype(jnp.bfloat16), own_rows, preferred_element_type=jnp.float32
    ).astype(jnp.bfloat16)
    packed_spot = jnp.sum(placer.astype(jnp.int32) * spot_index[None, :], axis=1)
    arrivals, arrival_spots = (
        lax.all_to_all(
            packed.reshape(n_dev, per_learner, feature_width),
            ("member", "tp"),
            split_axis=0,
            concat_axis=0,
            tiled=True,
        ),
        lax.all_to_all(
            packed_spot.reshape(n_dev, per_learner),
            ("member", "tp"),
            split_axis=0,
            concat_axis=0,
            tiled=True,
        ),
    )
    arrivals = arrivals.reshape(rows_here, feature_width)
    arrival_spots = arrival_spots.reshape(rows_here)
    settle = (jnp.arange(rows_here, dtype=jnp.int32)[:, None] == arrival_spots[None, :]).astype(
        jnp.bfloat16
    )
    imagined = jnp.dot(settle, arrivals, preferred_element_type=jnp.float32).astype(jnp.bfloat16)
    policy_normed = rms_scale(imagined.astype(jnp.float32), policy_gain).astype(jnp.bfloat16)
    action = jnp.tanh(jnp.dot(policy_normed, w_policy, preferred_element_type=jnp.float32)).astype(
        jnp.bfloat16
    )
    return (imagined, action)


def solution(mesh):
    in_specs = (
        P(("rep", "member", "tp"), None),
        P(("rep", "member", "tp"), None),
        P(("rep", "member", "tp")),
        P(),
        P("member", None, "tp"),
        P("member", "tp", None),
        P(),
        P(),
    )
    out_specs = (P(("rep", "member", "tp"), None), P(("rep", "member", "tp"), None))
    return jax.shard_map(local, mesh=mesh, in_specs=in_specs, out_specs=out_specs, check_vma=False)
```

profile of v0, /device:TPU:0, one launch (start us, length us, event | category | flops | bytes accessed | tf_op | source)
XLA Modules:
  0.0 330.6 jit_solution(9997030250772812439)
XLA Ops:
  7.2 0.9 fusion.38
  8.1 0.2 reduce_window_sum.23
  8.3 0.8 select_reduce_fusion
  9.1 0.7 multiply_add_fusion
  9.8 2.0 convolution_convert_fusion
  11.8 7.4 %all-to-all-start.1 = ((bf16[16,16,1024]{2,1,0:T(8,128)(2,1)}), bf16[16,16,1024]{2,1,0:T(8,128)(2,1)S(1)}, u32[]{:S(2)}, u32[]{:S(2)}) async-start(bf16[16,16,1024]{2,1,0:T(8,128)(2,1)} %bitcast.2), calls=%async_computation.1 | async-start | bytes 1048576 | tf_op jit(solution)/shard_map/all_to_all | solution.py:39
  19.3 0.7 constant_dynamic-slice_fusion
  20.0 14.9 %all-to-all-done.1 = bf16[16,16,1024]{2,1,0:T(8,128)(2,1)S(1)} async-done(((bf16[16,16,1024]{2,1,0:T(8,128)(2,1)}), bf16[16,16,1024]{2,1,0:T(8,128)(2,1)S(1)}, u32[]{:S(2)}, u32[]{:S(2)}) %all-to-all-start.1) | async-done | bytes 524320 | tf_op jit(solution)/shard_map/all_to_all | solution.py:39
  34.9 0.2 fusion.25
  35.1 0.2 fusion.27
  35.4 1.9 collective-permute-done
  37.3 1.1 pad_maximum_fusion
  38.5 79.5 %all-gather.2.cloned.1.call-done = bf16[2048,1024]{1,0:T(8,128)(2,1)} async-done(((bf16[512,1024]{1,0:T(8,128)(2,1)}), bf16[2048,1024]{1,0:T(8,128)(2,1)}) %all-gather.2.cloned.1.call-update) | async-done | bytes 4194320 | tf_op jit(solution)/shard_map/all_gather | solution.py:57
  118.0 10.6 %fusion.8 = f32[2048,1024]{1,0:T(8,128)} fusion(bf16[1,512,1024]{2,1,0:T(8,128)(2,1)S(1)} %copy-done, bf16[2048,1024]{1,0:T(8,128)(2,1)} %all-gather.2.cloned.1.call-done, bf16[1,1024,512]{2,1,0:T(8,128)(2,1)S(1)} %copy-done.2), kind=kOutput, calls=%fused_computation.9 | convolution fusion | flops 4304404480 | bytes 14680064 | tf_op jit(solution)/shard_map/dot_general | solution.py:63
  128.7 143.1 %reduce-scatter.2.cloned.1.call-done = f32[512,1024]{1,0:T(8,128)} async-done(((f32[2048,1024]{1,0:T(8,128)}), f32[512,1024]{1,0:T(8,128)}) %reduce-scatter.2.cloned.1.call-update) | async-done | bytes 2097168 | tf_op jit(solution)/shard_map/reduce_scatter | solution.py:62
  271.8 1.3 slice.9
  273.2 2.6 collective-permute-done.1
  275.9 2.2 fusion.17
  278.1 5.4 %all-to-all-start.2 = ((bf16[16,16,1024]{2,1,0:T(8,128)(2,1)}), bf16[16,16,1024]{2,1,0:T(8,128)(2,1)S(1)}, u32[]{:S(2)}, u32[]{:S(2)}) async-start(bf16[16,16,1024]{2,1,0:T(8,128)(2,1)} %bitcast.7), calls=%async_computation.3 | async-start | bytes 1048576 | tf_op jit(solution)/shard_map/all_to_all | solution.py:71
  283.6 0.2 reduce_window_sum.22
  283.8 0.2 select_reduce_fusion.2
  284.1 0.7 all_to_all.15
  284.8 14.4 %all-to-all-done.2 = bf16[16,16,1024]{2,1,0:T(8,128)(2,1)S(1)} async-done(((bf16[16,16,1024]{2,1,0:T(8,128)(2,1)}), bf16[16,16,1024]{2,1,0:T(8,128)(2,1)S(1)}, u32[]{:S(2)}, u32[]{:S(2)}) %all-to-all-start.2) | async-done | bytes 524320 | tf_op jit(solution)/shard_map/all_to_all | solution.py:71
  299.2 3.5 %all-to-all-start = ((s32[16,1,8]{2,1,0:T(1,128)}), s32[16,1,8]{2,1,0:T(1,128)S(1)}, u32[]{:S(2)}, u32[]{:S(2)}) async-start(s32[16,1,8]{2,1,0:T(1,128)} %bitcast), calls=%async_computation | async-start | bytes 16384 | tf_op jit(solution)/shard_map/all_to_all | solution.py:102
  302.7 1.1 fusion.14
  303.8 5.1 %all-to-all-done = s32[16,1,8]{2,1,0:T(1,128)S(1)} async-done(((s32[16,1,8]{2,1,0:T(1,128)}), s32[16,1,8]{2,1,0:T(1,128)S(1)}, u32[]{:S(2)}, u32[]{:S(2)}) %all-to-all-start) | async-done | bytes 544 | tf_op jit(solution)/shard_map/all_to_all | solution.py:102
  308.9 3.5 %all-to-all-start.3 = ((bf16[16,8,1024]{2,1,0:T(8,128)(2,1)}), bf16[16,8,1024]{2,1,0:T(8,128)(2,1)S(1)}, u32[]{:S(2)}, u32[]{:S(2)}) async-start(bf16[16,8,1024]{2,1,0:T(8,128)(2,1)} %fusion.14), calls=%async_computation.4 | async-start | bytes 524288 | tf_op jit(solution)/shard_map/all_to_all | solution.py:95
  312.5 0.5 broadcast.140
  313.0 0.7 reduce.4
  313.7 8.7 %all-to-all-done.3 = bf16[16,8,1024]{2,1,0:T(8,128)(2,1)S(1)} async-done(((bf16[16,8,1024]{2,1,0:T(8,128)(2,1)}), bf16[16,8,1024]{2,1,0:T(8,128)(2,1)S(1)}, u32[]{:S(2)}, u32[]{:S(2)}) %all-to-all-start.3) | async-done | bytes 262176 | tf_op jit(solution)/shard_map/all_to_all | solution.py:95
  322.5 0.3 fusion.28
  322.8 0.9 fusion.15
  (26 shorter events, 0.7 us)
Async XLA Ops:
  7.2 110.8 %copy-start = (bf16[1,512,1024]{2,1,0:T(8,128)(2,1)S(1)}, bf16[1,512,1024]{2,1,0:T(8,128)(2,1)}, u32[]{:S(2)}) copy-start(bf16[1,512,1024]{2,1,0:T(8,128)(2,1)} %param.13) | copy-start | bytes 3145732
  7.2 110.8 %copy-start.2 = (bf16[1,1024,512]{2,1,0:T(8,128)(2,1)S(1)}, bf16[1,1024,512]{2,1,0:T(8,128)(2,1)}, u32[]{:S(2)}) copy-start(bf16[1,1024,512]{2,1,0:T(8,128)(2,1)} %param.12) | copy-start | bytes 3145732
  11.8 23.1 %all-to-all-start.1 = ((bf16[16,16,1024]{2,1,0:T(8,128)(2,1)}), bf16[16,16,1024]{2,1,0:T(8,128)(2,1)S(1)}, u32[]{:S(2)}, u32[]{:S(2)}) async-start(bf16[16,16,1024]{2,1,0:T(8,128)(2,1)} %bitcast.2), calls=%async_computation.1 | async-start | bytes 1048576 | tf_op jit(solution)/shard_map/all_to_all | solution.py:39
  19.2 98.8 %all-gather.2.cloned.1.call-start = ((), (), s32[]{:S(2)}) async-start(), calls=%async_computation.5 | async-start | bytes 5242880 | tf_op jit(solution)/shard_map/all_gather | solution.py:57
  35.3 2.0 collective-permute-start
  38.4 233.4 %reduce-scatter.2.cloned.1.call-start = ((), (), s32[]{:S(2)}) async-start(), calls=%async_computation.6 | async-start | bytes 10485760 | tf_op jit(solution)/shard_map/reduce_scatter | solution.py:62
  128.6 154.9 %copy-start.5 = (s32[128]{0:T(128)S(1)}, s32[128]{0:T(128)}, u32[]{:S(2)}) copy-start(s32[128]{0:T(128)} %param.10) | copy-start | bytes 1540
  128.6 194.2 %copy-start.3 = (bf16[1024,128]{1,0:T(8,128)(2,1)S(1)}, bf16[1024,128]{1,0:T(8,128)(2,1)}, u32[]{:S(2)}) copy-start(bf16[1024,128]{1,0:T(8,128)(2,1)} %param.15) | copy-start | bytes 786436
  128.6 194.2 %copy-start.4 = (f32[1024]{0:T(1024)S(1)}, f32[1024]{0:T(1024)}, u32[]{:S(2)}) copy-start(f32[1024]{0:T(1024)} %param.14) | copy-start | bytes 12292
  273.1 2.7 collective-permute-start.1
  278.1 21.1 %all-to-all-start.2 = ((bf16[16,16,1024]{2,1,0:T(8,128)(2,1)}), bf16[16,16,1024]{2,1,0:T(8,128)(2,1)S(1)}, u32[]{:S(2)}, u32[]{:S(2)}) async-start(bf16[16,16,1024]{2,1,0:T(8,128)(2,1)} %bitcast.7), calls=%async_computation.3 | async-start | bytes 1048576 | tf_op jit(solution)/shard_map/all_to_all | solution.py:71
  299.2 9.7 %all-to-all-start = ((s32[16,1,8]{2,1,0:T(1,128)}), s32[16,1,8]{2,1,0:T(1,128)S(1)}, u32[]{:S(2)}, u32[]{:S(2)}) async-start(s32[16,1,8]{2,1,0:T(1,128)} %bitcast), calls=%async_computation | async-start | bytes 16384 | tf_op jit(solution)/shard_map/all_to_all | solution.py:102
  308.9 13.6 %all-to-all-start.3 = ((bf16[16,8,1024]{2,1,0:T(8,128)(2,1)}), bf16[16,8,1024]{2,1,0:T(8,128)(2,1)S(1)}, u32[]{:S(2)}, u32[]{:S(2)}) async-start(bf16[16,8,1024]{2,1,0:T(8,128)(2,1)} %fusion.14), calls=%async_computation.4 | async-start | bytes 524288 | tf_op jit(solution)/shard_map/all_to_all | solution.py:95
  322.8 1.0 copy-start.1
Sparse Core Ops, SparseCore 0:
  38.5 79.4 all-gather.1
  128.7 143.0 reduce-scatter.1
where the time goes:
time: 331 us
  waiting for transfers between devices  270 us (82%)
  starting transfers between devices  20 us (6%)
  matrix products  15 us (5%)
  between operations  14.3 us (4%)
  other arithmetic  7.45 us (2%)
  local copies, waits for them, and re-layouts  3.45 us (1%)
    reduce_scatter x1, waiting for transfers between devices, local(): lax.psum_scatter(jnp.dot(hidden, down_local, preferred_element_type=jnp.f...  143 us
    all_gather x1, waiting for transfers between devices, local(): lax.all_gather(both_rows, 'tp', axis=0, tiled=True)  79.5 us
    all_to_all x1, waiting for transfers between devices, local(): lax.all_to_all(outgoing.reshape(n_dev, slot_count, feature_width), ('memb...  14.9 us
    all_to_all x1, waiting for transfers between devices, local(): lax.all_to_all(predicted.reshape(n_dev, slot_count, feature_width), ('mem...  14.4 us
    dot_general x1, matrix products, local(): jnp.dot(hidden, down_local, preferred_element_type=jnp.float32)  10.6 us
    all_to_all x1, waiting for transfers between devices, local(): lax.all_to_all(packed.reshape(n_dev, per_learner, feature_width), ('membe...  8.74 us
    all_to_all x1, starting transfers between devices, local(): lax.all_to_all(outgoing.reshape(n_dev, slot_count, feature_width), ('memb...  7.39 us
  transfers between devices with their start and end apart: 8, of which 8 were waited for; matrix products, arithmetic and copies ran while one was open for 1% of the time, Pallas kernels for 0%

commit v1 on v0

--- a/solution.py
+++ b/solution.py
@@ -2,6 +2,22 @@
 import jax.numpy as jnp
 from jax import lax
 from jax.sharding import PartitionSpec as P
+
+
+def exchange_in_pairs(x, axis, split, join):
+    ways, here = (lax.axis_size(axis), lax.axis_index(axis))
+    width = x.shape[split] // ways
+    dims = list(x.shape)
+    dims[split] = width
+    height = dims[join]
+    dims[join] = height * ways
+    full = jnp.zeros(dims, x.dtype)
+    for mask in range(ways):
+        part = lax.dynamic_slice_in_dim(x, (here ^ mask) * width, width, axis=split)
+        if mask:
+            part = lax.ppermute(part, axis, [(d, d ^ mask) for d in range(ways)])
+        full = lax.dynamic_update_slice_in_dim(full, part, (here ^ mask) * height, axis=join)
+    return full
 
 
 def from_partner(value, axis, distance):
@@ -36,12 +52,8 @@
         jnp.bfloat16
     )
     outgoing = jnp.dot(picker, states, preferred_element_type=jnp.float32).astype(jnp.bfloat16)
-    arrived = lax.all_to_all(
-        outgoing.reshape(n_dev, slot_count, feature_width),
-        ("member", "tp"),
-        split_axis=0,
-        concat_axis=0,
-        tiled=True,
+    arrived = exchange_in_pairs(
+        outgoing.reshape(n_dev, slot_count, feature_width), ("member", "tp"), 0, 0
     )
     arrived = arrived.reshape(n_dev * slot_count, feature_width)
     arrived_count = arrived.shape[0]

time: 331 us -> 368 us (1.11)
  starting transfers between devices: 20 us -> 43.4 us
  waiting for transfers between devices: 270 us -> 284 us
    ppermute x0 -> x15, starting transfers between devices: none -> 30.8 us  [exchange_in_pairs(): part = lax.ppermute(part, axis, [(d, d ^ mask) for d in range(ways)])]
    ppermute x0 -> x15, waiting for transfers between devices: none -> 26.1 us  [exchange_in_pairs(): part = lax.ppermute(part, axis, [(d, d ^ mask) for d in range(ways)])]
    all_to_all x1 -> x0, waiting for transfers between devices: 14.9 us -> none  [local(): lax.all_to_all(outgoing.reshape(n_dev, slot_count, feature_width), ('memb...]
    all_to_all x1 -> x0, starting transfers between devices: 7.39 us -> none  [local(): lax.all_to_all(outgoing.reshape(n_dev, slot_count, feature_width), ('memb...]
  transfers between devices with their start and end apart: 8 -> 22, of which waited for: 8 -> 18; matrix products, arithmetic and copies ran while one was open for 1% -> 1% of each run, Pallas kernels for 0% -> 0%
where the time goes in v1:
time: 368 us
  waiting for transfers between devices  284 us (77%)
  starting transfers between devices  43.4 us (12%)
  between operations  14.5 us (4%)
  matrix products  14.2 us (4%)
  other arithmetic  7.47 us (2%)
  local copies, waits for them, and re-layouts  3.69 us (1%)
    reduce_scatter x1, waiting for transfers between devices, local(): lax.psum_scatter(jnp.dot(hidden, down_local, preferred_element_type=jnp.f...  143 us
    all_gather x1, waiting for transfers between devices, local(): lax.all_gather(both_rows, 'tp', axis=0, tiled=True)  82.3 us
    ppermute x15, starting transfers between devices, exchange_in_pairs(): part = lax.ppermute(part, axis, [(d, d ^ mask) for d in range(ways)])  30.8 us
    ppermute x15, waiting for transfers between devices, exchange_in_pairs(): part = lax.ppermute(part, axis, [(d, d ^ mask) for d in range(ways)])  26.1 us
    all_to_all x1, waiting for transfers between devices, local(): lax.all_to_all(predicted.reshape(n_dev, slot_count, feature_width), ('mem...  14.4 us
    dot_general x1, matrix products, local(): jnp.dot(hidden, down_local, preferred_element_type=jnp.float32)  10.6 us
    all_to_all x1, waiting for transfers between devices, local(): lax.all_to_all(packed.reshape(n_dev, per_learner, feature_width), ('membe...  8.74 us
  transfers between devices with their start and end apart: 22, of which 18 were waited for; matrix products, arithmetic and copies ran while one was open for 1% of the time, Pallas kernels for 0%

profile of v1, /device:TPU:0, one launch (start us, length us, event | category | flops | bytes accessed | tf_op | source)
XLA Modules:
  0.0 367.6 jit_solution(13228797325757676176)
XLA Ops:
  11.4 5.5 %collective-permute-start.14 = (bf16[1,16,1024]{2,1,0:T(8,128)(2,1)S(1)}, bf16[1,16,1024]{2,1,0:T(8,128)(2,1)S(1)}, u32[]{:S(2)}, u32[]{:S(2)}) collective-permute-start(bf16[1,16,1024]{2,1,0:T(8,128)(2,1)S(1)} %get-tuple-element.2), channel_id=1, source_target_pairs={{0,15},{1,14},{2,13},{3,12},{4,11},{5,10},{6,9},{7,8},{8,7},{9,6},... | collective-permute-start | bytes 98312 | tf_op jit(solution)/shard_map/ppermute | solution.py:18
  16.9 1.4 collective-permute-start.12
  18.7 1.4 collective-permute-start
  20.8 1.9 collective-permute-done
  22.7 2.7 collective-permute-start.1
  25.4 2.1 collective-permute-done.1
  27.6 3.9 %collective-permute-start.2 = (bf16[1,16,1024]{2,1,0:T(8,128)(2,1)S(1)}, bf16[1,16,1024]{2,1,0:T(8,128)(2,1)S(1)}, u32[]{:S(2)}, u32[]{:S(2)}) collective-permute-start(bf16[1,16,1024]{2,1,0:T(8,128)(2,1)S(1)} %get-tuple-element.14), channel_id=1, source_target_pairs={{0,3},{1,2},{2,1},{3,0},{4,7},{5,6},{6,5},{7,4},{8,11},{9,10},{10,... | collective-permute-start | bytes 98312 | tf_op jit(solution)/shard_map/ppermute | solution.py:18
  31.5 1.9 collective-permute-done.2
  34.6 3.3 collective-permute-done.4
  37.9 2.4 collective-permute-start.5
  40.3 1.9 collective-permute-done.5
  42.2 4.1 %collective-permute-start.6 = (bf16[1,16,1024]{2,1,0:T(8,128)(2,1)S(1)}, bf16[1,16,1024]{2,1,0:T(8,128)(2,1)S(1)}, u32[]{:S(2)}, u32[]{:S(2)}) collective-permute-start(bf16[1,16,1024]{2,1,0:T(8,128)(2,1)S(1)} %get-tuple-element.10), channel_id=1, source_target_pairs={{0,7},{1,6},{2,5},{3,4},{4,3},{5,2},{6,1},{7,0},{8,15},{9,14},{10,... | collective-permute-start | bytes 98312 | tf_op jit(solution)/shard_map/ppermute | solution.py:18
  46.3 1.6 collective-permute-done.6
  47.9 1.5 collective-permute-start.7
  49.4 2.4 collective-permute-done.7
  52.1 4.5 %collective-permute-done.8 = bf16[1,16,1024]{2,1,0:T(8,128)(2,1)S(1)} collective-permute-done((bf16[1,16,1024]{2,1,0:T(8,128)(2,1)S(1)}, bf16[1,16,1024]{2,1,0:T(8,128)(2,1)S(1)}, u32[]{:S(2)}, u32[]{:S(2)}) %collective-permute-start.8) | collective-permute-done | bytes 32800 | tf_op jit(solution)/shard_map/ppermute | solution.py:18
  56.7 2.4 collective-permute-start.9
  59.1 3.3 collective-permute-done.9
  62.4 4.8 %collective-permute-start.10 = (bf16[1,16,1024]{2,1,0:T(8,128)(2,1)S(1)}, bf16[1,16,1024]{2,1,0:T(8,128)(2,1)S(1)}, u32[]{:S(2)}, u32[]{:S(2)}) collective-permute-start(bf16[1,16,1024]{2,1,0:T(8,128)(2,1)S(1)} %get-tuple-element.6), channel_id=1, source_target_pairs={{0,11},{1,10},{2,9},{3,8},{4,15},{5,14},{6,13},{7,12},{8,3},{9,2},... | collective-permute-start | bytes 98312 | tf_op jit(solution)/shard_map/ppermute | solution.py:18
  67.1 1.9 collective-permute-done.10
  69.7 1.9 collective-permute-done.15
  72.7 82.3 %all-gather.2.cloned.1.call-done = bf16[2048,1024]{1,0:T(8,128)(2,1)} async-done(((bf16[512,1024]{1,0:T(8,128)(2,1)}), bf16[2048,1024]{1,0:T(8,128)(2,1)}) %all-gather.2.cloned.1.call-update) | async-done | bytes 4194320 | tf_op jit(solution)/shard_map/all_gather | solution.py:69
  155.0 10.6 %fusion.8 = f32[2048,1024]{1,0:T(8,128)} fusion(bf16[1,512,1024]{2,1,0:T(8,128)(2,1)S(1)} %copy-done, bf16[2048,1024]{1,0:T(8,128)(2,1)} %all-gather.2.cloned.1.call-done, bf16[1,1024,512]{2,1,0:T(8,128)(2,1)S(1)} %copy-done.2), kind=kOutput, calls=%fused_computation.9 | convolution fusion | flops 4304404480 | bytes 14680064 | tf_op jit(solution)/shard_map/dot_general | solution.py:75
  165.6 143.1 %reduce-scatter.2.cloned.1.call-done = f32[512,1024]{1,0:T(8,128)} async-done(((f32[2048,1024]{1,0:T(8,128)}), f32[512,1024]{1,0:T(8,128)}) %reduce-scatter.2.cloned.1.call-update) | async-done | bytes 2097168 | tf_op jit(solution)/shard_map/reduce_scatter | solution.py:74
  310.2 2.6 collective-permute-done.16
  312.8 2.2 fusion.17
  315.1 5.4 %all-to-all-start.1 = ((bf16[16,16,1024]{2,1,0:T(8,128)(2,1)}), bf16[16,16,1024]{2,1,0:T(8,128)(2,1)S(1)}, u32[]{:S(2)}, u32[]{:S(2)}) async-start(bf16[16,16,1024]{2,1,0:T(8,128)(2,1)} %bitcast.7), calls=%async_computation.2 | async-start | bytes 1048576 | tf_op jit(solution)/shard_map/all_to_all | solution.py:83
  321.8 14.4 %all-to-all-done.1 = bf16[16,16,1024]{2,1,0:T(8,128)(2,1)S(1)} async-done(((bf16[16,16,1024]{2,1,0:T(8,128)(2,1)}), bf16[16,16,1024]{2,1,0:T(8,128)(2,1)S(1)}, u32[]{:S(2)}, u32[]{:S(2)}) %all-to-all-start.1) | async-done | bytes 524320 | tf_op jit(solution)/shard_map/all_to_all | solution.py:83
  336.2 3.5 all-to-all-start
  340.8 5.1 %all-to-all-done = s32[16,1,8]{2,1,0:T(1,128)S(1)} async-done(((s32[16,1,8]{2,1,0:T(1,128)}), s32[16,1,8]{2,1,0:T(1,128)S(1)}, u32[]{:S(2)}, u32[]{:S(2)}) %all-to-all-start) | async-done | bytes 544 | tf_op jit(solution)/shard_map/all_to_all | solution.py:114
  345.9 3.5 all-to-all-start.2
  350.7 8.7 %all-to-all-done.2 = bf16[16,8,1024]{2,1,0:T(8,128)(2,1)S(1)} async-done(((bf16[16,8,1024]{2,1,0:T(8,128)(2,1)}), bf16[16,8,1024]{2,1,0:T(8,128)(2,1)S(1)}, u32[]{:S(2)}, u32[]{:S(2)}) %all-to-all-start.2) | async-done | bytes 262176 | tf_op jit(solution)/shard_map/all_to_all | solution.py:107
  (68 shorter events, 14.7 us)
Async XLA Ops:
  7.2 147.8 %copy-start = (bf16[1,512,1024]{2,1,0:T(8,128)(2,1)S(1)}, bf16[1,512,1024]{2,1,0:T(8,128)(2,1)}, u32[]{:S(2)}) copy-start(bf16[1,512,1024]{2,1,0:T(8,128)(2,1)} %param.13) | copy-start | bytes 3145732
  7.2 147.8 %all-gather.2.cloned.1.call-start = ((), (), s32[]{:S(2)}) async-start(), calls=%async_computation.4 | async-start | bytes 5242880 | tf_op jit(solution)/shard_map/all_gather | solution.py:69
  8.1 146.9 %copy-start.2 = (bf16[1,1024,512]{2,1,0:T(8,128)(2,1)S(1)}, bf16[1,1024,512]{2,1,0:T(8,128)(2,1)}, u32[]{:S(2)}) copy-start(bf16[1,1024,512]{2,1,0:T(8,128)(2,1)} %param.12) | copy-start | bytes 3145732
  11.4 57.7 %collective-permute-start.14 = (bf16[1,16,1024]{2,1,0:T(8,128)(2,1)S(1)}, bf16[1,16,1024]{2,1,0:T(8,128)(2,1)S(1)}, u32[]{:S(2)}, u32[]{:S(2)}) collective-permute-start(bf16[1,16,1024]{2,1,0:T(8,128)(2,1)S(1)} %get-tuple-element.2), channel_id=1, source_target_pairs={{0,15},{1,14},{2,13},{3,12},{4,11},{5,10},{6,9},{7,8},{8,7},{9,6},... | collective-permute-start | bytes 98312 | tf_op jit(solution)/shard_map/ppermute | solution.py:18
  16.9 52.2 %collective-permute-start.13 = (bf16[1,16,1024]{2,1,0:T(8,128)(2,1)S(1)}, bf16[1,16,1024]{2,1,0:T(8,128)(2,1)S(1)}, u32[]{:S(2)}, u32[]{:S(2)}) collective-permute-start(bf16[1,16,1024]{2,1,0:T(8,128)(2,1)S(1)} %get-tuple-element.3), channel_id=1, source_target_pairs={{0,14},{1,15},{2,12},{3,13},{4,10},{5,11},{6,8},{7,9},{8,6},{9,7},... | collective-permute-start | bytes 98312 | tf_op jit(solution)/shard_map/ppermute | solution.py:18
  16.9 52.1 %collective-permute-start.12 = (bf16[1,16,1024]{2,1,0:T(8,128)(2,1)S(1)}, bf16[1,16,1024]{2,1,0:T(8,128)(2,1)S(1)}, u32[]{:S(2)}, u32[]{:S(2)}) collective-permute-start(bf16[1,16,1024]{2,1,0:T(8,128)(2,1)S(1)} %get-tuple-element.4), channel_id=1, source_target_pairs={{0,13},{1,12},{2,15},{3,14},{4,9},{5,8},{6,11},{7,10},{8,5},{9,4},... | collective-permute-start | bytes 98312 | tf_op jit(solution)/shard_map/ppermute | solution.py:18
  18.3 50.7 %collective-permute-start.11 = (bf16[1,16,1024]{2,1,0:T(8,128)(2,1)S(1)}, bf16[1,16,1024]{2,1,0:T(8,128)(2,1)S(1)}, u32[]{:S(2)}, u32[]{:S(2)}) collective-permute-start(bf16[1,16,1024]{2,1,0:T(8,128)(2,1)S(1)} %get-tuple-element.5), channel_id=1, source_target_pairs={{0,12},{1,13},{2,14},{3,15},{4,8},{5,9},{6,10},{7,11},{8,4},{9,5},... | collective-permute-start | bytes 98312 | tf_op jit(solution)/shard_map/ppermute | solution.py:18
  18.7 4.0 %collective-permute-start = (bf16[1,16,1024]{2,1,0:T(8,128)(2,1)S(1)}, bf16[1,16,1024]{2,1,0:T(8,128)(2,1)S(1)}, u32[]{:S(2)}, u32[]{:S(2)}) collective-permute-start(bf16[1,16,1024]{2,1,0:T(8,128)(2,1)S(1)} %get-tuple-element.16), channel_id=1, source_target_pairs={{0,1},{1,0},{2,3},{3,2},{4,5},{5,4},{6,7},{7,6},{8,9},{9,8},{10,11... | collective-permute-start | bytes 98312 | tf_op jit(solution)/shard_map/ppermute | solution.py:18
  22.7 4.8 %collective-permute-start.1 = (bf16[1,16,1024]{2,1,0:T(8,128)(2,1)S(1)}, bf16[1,16,1024]{2,1,0:T(8,128)(2,1)S(1)}, u32[]{:S(2)}, u32[]{:S(2)}) collective-permute-start(bf16[1,16,1024]{2,1,0:T(8,128)(2,1)S(1)} %get-tuple-element.15), channel_id=1, source_target_pairs={{0,2},{1,3},{2,0},{3,1},{4,6},{5,7},{6,4},{7,5},{8,10},{9,11},{10,... | collective-permute-start | bytes 98312 | tf_op jit(solution)/shard_map/ppermute | solution.py:18
  27.6 5.8 %collective-permute-start.2 = (bf16[1,16,1024]{2,1,0:T(8,128)(2,1)S(1)}, bf16[1,16,1024]{2,1,0:T(8,128)(2,1)S(1)}, u32[]{:S(2)}, u32[]{:S(2)}) collective-permute-start(bf16[1,16,1024]{2,1,0:T(8,128)(2,1)S(1)} %get-tuple-element.14), channel_id=1, source_target_pairs={{0,3},{1,2},{2,1},{3,0},{4,7},{5,6},{6,5},{7,4},{8,11},{9,10},{10,... | collective-permute-start | bytes 98312 | tf_op jit(solution)/shard_map/ppermute | solution.py:18
  33.4 1.2 collective-permute-start.3
  34.6 3.3 collective-permute-start.4
  37.9 4.2 %collective-permute-start.5 = (bf16[1,16,1024]{2,1,0:T(8,128)(2,1)S(1)}, bf16[1,16,1024]{2,1,0:T(8,128)(2,1)S(1)}, u32[]{:S(2)}, u32[]{:S(2)}) collective-permute-start(bf16[1,16,1024]{2,1,0:T(8,128)(2,1)S(1)} %get-tuple-element.11), channel_id=1, source_target_pairs={{0,6},{1,7},{2,4},{3,5},{4,2},{5,3},{6,0},{7,1},{8,14},{9,15},{10,... | collective-permute-start | bytes 98312 | tf_op jit(solution)/shard_map/ppermute | solution.py:18
  42.2 5.7 %collective-permute-start.6 = (bf16[1,16,1024]{2,1,0:T(8,128)(2,1)S(1)}, bf16[1,16,1024]{2,1,0:T(8,128)(2,1)S(1)}, u32[]{:S(2)}, u32[]{:S(2)}) collective-permute-start(bf16[1,16,1024]{2,1,0:T(8,128)(2,1)S(1)} %get-tuple-element.10), channel_id=1, source_target_pairs={{0,7},{1,6},{2,5},{3,4},{4,3},{5,2},{6,1},{7,0},{8,15},{9,14},{10,... | collective-permute-start | bytes 98312 | tf_op jit(solution)/shard_map/ppermute | solution.py:18
  47.9 3.9 %collective-permute-start.7 = (bf16[1,16,1024]{2,1,0:T(8,128)(2,1)S(1)}, bf16[1,16,1024]{2,1,0:T(8,128)(2,1)S(1)}, u32[]{:S(2)}, u32[]{:S(2)}) collective-permute-start(bf16[1,16,1024]{2,1,0:T(8,128)(2,1)S(1)} %get-tuple-element.9), channel_id=1, source_target_pairs={{0,8},{1,9},{2,10},{3,11},{4,12},{5,13},{6,14},{7,15},{8,0},{9,1},... | collective-permute-start | bytes 98312 | tf_op jit(solution)/shard_map/ppermute | solution.py:18
  51.8 4.8 %collective-permute-start.8 = (bf16[1,16,1024]{2,1,0:T(8,128)(2,1)S(1)}, bf16[1,16,1024]{2,1,0:T(8,128)(2,1)S(1)}, u32[]{:S(2)}, u32[]{:S(2)}) collective-permute-start(bf16[1,16,1024]{2,1,0:T(8,128)(2,1)S(1)} %get-tuple-element.8), channel_id=1, source_target_pairs={{0,9},{1,8},{2,11},{3,10},{4,13},{5,12},{6,15},{7,14},{8,1},{9,0},... | collective-permute-start | bytes 98312 | tf_op jit(solution)/shard_map/ppermute | solution.py:18
  56.7 5.7 %collective-permute-start.9 = (bf16[1,16,1024]{2,1,0:T(8,128)(2,1)S(1)}, bf16[1,16,1024]{2,1,0:T(8,128)(2,1)S(1)}, u32[]{:S(2)}, u32[]{:S(2)}) collective-permute-start(bf16[1,16,1024]{2,1,0:T(8,128)(2,1)S(1)} %get-tuple-element.7), channel_id=1, source_target_pairs={{0,10},{1,11},{2,8},{3,9},{4,14},{5,15},{6,12},{7,13},{8,2},{9,3},... | collective-permute-start | bytes 98312 | tf_op jit(solution)/shard_map/ppermute | solution.py:18
  62.4 6.7 %collective-permute-start.10 = (bf16[1,16,1024]{2,1,0:T(8,128)(2,1)S(1)}, bf16[1,16,1024]{2,1,0:T(8,128)(2,1)S(1)}, u32[]{:S(2)}, u32[]{:S(2)}) collective-permute-start(bf16[1,16,1024]{2,1,0:T(8,128)(2,1)S(1)} %get-tuple-element.6), channel_id=1, source_target_pairs={{0,11},{1,10},{2,9},{3,8},{4,15},{5,14},{6,13},{7,12},{8,3},{9,2},... | collective-permute-start | bytes 98312 | tf_op jit(solution)/shard_map/ppermute | solution.py:18
  69.6 2.0 collective-permute-start.15
  72.7 236.1 %reduce-scatter.2.cloned.1.call-start = ((), (), s32[]{:S(2)}) async-start(), calls=%async_computation.5 | async-start | bytes 10485760 | tf_op jit(solution)/shard_map/reduce_scatter | solution.py:74
  165.6 194.2 %copy-start.3 = (bf16[1024,128]{1,0:T(8,128)(2,1)S(1)}, bf16[1024,128]{1,0:T(8,128)(2,1)}, u32[]{:S(2)}) copy-start(bf16[1024,128]{1,0:T(8,128)(2,1)} %param.15) | copy-start | bytes 786436
  165.6 194.2 %copy-start.4 = (f32[1024]{0:T(1024)S(1)}, f32[1024]{0:T(1024)}, u32[]{:S(2)}) copy-start(f32[1024]{0:T(1024)} %param.14) | copy-start | bytes 12292
  310.1 2.7 collective-permute-start.16
  315.1 21.1 %all-to-all-start.1 = ((bf16[16,16,1024]{2,1,0:T(8,128)(2,1)}), bf16[16,16,1024]{2,1,0:T(8,128)(2,1)S(1)}, u32[]{:S(2)}, u32[]{:S(2)}) async-start(bf16[16,16,1024]{2,1,0:T(8,128)(2,1)} %bitcast.7), calls=%async_computation.2 | async-start | bytes 1048576 | tf_op jit(solution)/shard_map/all_to_all | solution.py:83
  336.2 9.7 %all-to-all-start = ((s32[16,1,8]{2,1,0:T(1,128)}), s32[16,1,8]{2,1,0:T(1,128)S(1)}, u32[]{:S(2)}, u32[]{:S(2)}) async-start(s32[16,1,8]{2,1,0:T(1,128)} %bitcast), calls=%async_computation | async-start | bytes 16384 | tf_op jit(solution)/shard_map/all_to_all | solution.py:114
  345.9 13.6 %all-to-all-start.2 = ((bf16[16,8,1024]{2,1,0:T(8,128)(2,1)}), bf16[16,8,1024]{2,1,0:T(8,128)(2,1)S(1)}, u32[]{:S(2)}, u32[]{:S(2)}) async-start(bf16[16,8,1024]{2,1,0:T(8,128)(2,1)} %fusion.14), calls=%async_computation.3 | async-start | bytes 524288 | tf_op jit(solution)/shard_map/all_to_all | solution.py:107
  359.8 1.0 copy-start.1
Sparse Core Ops, SparseCore 0:
  72.8 82.1 all-gather.1
  165.7 143.0 reduce-scatter.1
